TPU v7x, 32 devices: a whole 2x2x4 slice. The times are simulated.
32 devices in a mesh: grp: 4 (over z), emb: 8 (over y, x, core).
Axes of the slice: x: 2, y: 2, z: 4, core: 2. Of those that a mesh axis runs over, the one named last changes fastest.
Arguments:
- bottom_out: bfloat16 [4096, 128], P(('grp', 'emb')), may hold values from -6 to 6
- owner_ids: int32 [106496, 1], P(('grp', 'emb')), may hold values from 0 to 7; in each aligned block of 3328 rows (0 to 3327, 3328 to 6655, ...) at most 624 rows name the same one
- row_ids: int32 [4096, 26], P(('grp', 'emb')), may hold values from 0 to 95
- positions: int32 [4096], P(('grp', 'emb')), may hold values from 0 to 15
- labels: int32 [4096], P(('grp', 'emb')), may hold values 0 or 1
- tables: bfloat16 [26, 768, 128], P(None, 'emb'), may hold values from -6 to 6
- cross_down: bfloat16 [3456, 512], replicated, may hold values from -0.109375 to 0.109375
- cross_up: bfloat16 [512, 3456], replicated, may hold values from -0.25 to 0.25
- cross_bias: float32 [3456], replicated, may hold values from -3 to 3
- out_weight: bfloat16 [3456], replicated, may hold values from -0.109375 to 0.109375
- position_bias: float32 [16], replicated, may hold values from -2 to 2
Outputs:
- table_grad: float32 [26, 768, 128], P(None, 'emb')
- bottom_grad: bfloat16 [4096, 128], P(('grp', 'emb'))
- bias_grad: float32 [3456], replicated
Inputs may be any that keep to these rules, and one draw needn't show every extreme that they name: `owner_ids`: in every aligned block of 3328 lookups (the lookups of one device) no owner is named more than 624 times, and in some block one owner is named exactly 624 times.
All inputs are finite; a program needn't handle non-finite values. No bound on the sum of `labels` on one device may be relied on, other than what follows from the above.
Results may differ from a plain program's by a relative error of at most 0.0085.
Values may be sent and summed in bfloat16 or wider, within the bound.
No kernel may reach another device: no remote copies, remote signals or barrier semaphores. Data moves between devices by JAX's collectives and lax.ppermute only.
A program may use at most 64 MiB of HBM per device.

v0:
```python
import jax
import jax.numpy as jnp
from jax import lax
from jax.sharding import PartitionSpec as P


def local(
    bottom_out,
    owner_ids,
    row_ids,
    positions,
    labels,
    tables,
    cross_down,
    cross_up,
    cross_bias,
    out_weight,
    position_bias,
):
    sample_count, table_count = row_ids.shape
    rows_local = tables.shape[1]
    row_width = tables.shape[2]
    owner_count = lax.axis_size("emb")
    capacity = 3 * sample_count * table_count // (2 * owner_count)
    lookup_count = sample_count * table_count
    owners = owner_ids.reshape(sample_count, table_count)
    flat_owner = owners.reshape(-1)
    local_grid = jnp.arange(table_count, dtype=jnp.int32)[None, :] * rows_local + row_ids
    local_index = local_grid.reshape(-1)
    owner_marks = (flat_owner[:, None] == jnp.arange(owner_count, dtype=jnp.int32)[None, :]).astype(
        jnp.int32
    )
    ranking = jnp.cumsum(owner_marks, axis=0) - 1
    slot_index = jnp.sum(ranking * owner_marks, axis=1)
    buffer_place = flat_owner * capacity + slot_index
    flat_table = tables.reshape(table_count * rows_local, row_width)
    request = jnp.zeros((owner_count * capacity,), jnp.int32).at[buffer_place].set(local_index)
    request = request.reshape(owner_count, capacity)
    received = lax.all_to_all(request, "emb", split_axis=0, concat_axis=0, tiled=True)
    fetched = flat_table[received]
    arrived = lax.all_to_all(fetched, "emb", split_axis=0, concat_axis=0, tiled=True)
    pooled = arrived.reshape(owner_count * capacity, row_width)[buffer_place].reshape(
        sample_count, table_count * row_width
    )
    first = jnp.concatenate([bottom_out, pooled], axis=1)
    first_wide = first.astype(jnp.float32)
    weight_row = out_weight.astype(jnp.float32)
    reduced = jnp.dot(first, cross_down, preferred_element_type=jnp.float32).astype(jnp.bfloat16)
    gate_scale = jnp.dot(reduced, cross_up, preferred_element_type=jnp.float32) + cross_bias
    crossed = first_wide * gate_scale + first_wide
    position_marks = (
        positions[:, None] == jnp.arange(position_bias.shape[0], dtype=jnp.int32)[None, :]
    ).astype(jnp.float32)
    logit = jnp.sum(crossed * weight_row[None, :], axis=1) + jnp.sum(
        position_marks * position_bias[None, :], axis=1
    )
    err = jax.nn.sigmoid(logit) - labels.astype(jnp.float32)
    cotangent = err[:, None] * weight_row[None, :]
    scaled = cotangent * first_wide
    down_grad = lax.dot_general(
        scaled.astype(jnp.bfloat16),
        cross_up,
        (((1,), (1,)), ((), ())),
        preferred_element_type=jnp.float32,
    ).astype(jnp.bfloat16)
    back_term = lax.dot_general(
        down_grad, cross_down, (((1,), (1,)), ((), ())), preferred_element_type=jnp.float32
    )
    input_grad = (cotangent * (gate_scale + 1.0) + back_term).astype(jnp.bfloat16)
    bottom_grad = input_grad[:, :row_width]
    row_grads = input_grad[:, row_width:].reshape(lookup_count, row_width)
    outgoing = (
        jnp.zeros((owner_count * capacity, row_width), jnp.bfloat16).at[buffer_place].set(row_grads)
    )
    incoming = lax.all_to_all(
        outgoing.reshape(owner_count, capacity, row_width),
        "emb",
        split_axis=0,
        concat_axis=0,
        tiled=True,
    )
    local_grad = (
        jnp.zeros((table_count * rows_local, row_width), jnp.float32)
        .at[received.reshape(-1)]
        .add(incoming.reshape(owner_count * capacity, row_width).astype(jnp.float32))
    )
    summed_grad = lax.psum(local_grad.astype(jnp.bfloat16), "grp").astype(jnp.float32)
    table_grad = summed_grad.reshape(table_count, rows_local, row_width)
    bias_local = jnp.sum(scaled, axis=0)
    bias_grad = lax.psum(bias_local, ("grp", "emb"))
    return (table_grad, bottom_grad, bias_grad)


def solution(mesh):
    placed = (
        P(("grp", "emb"), None),
        P(("grp", "emb"), None),
        P(("grp", "emb"), None),
        P(("grp", "emb")),
        P(("grp", "emb")),
        P(None, "emb", None),
        P(),
        P(),
        P(),
        P(),
        P(),
    )
    return jax.shard_map(
        local,
        mesh=mesh,
        in_specs=placed,
        out_specs=(P(None, "emb", None), P(("grp", "emb"), None), P()),
        check_vma=False,
    )
```

profile of v0, /device:TPU:0, one launch (start us, length us, event | category | flops | bytes accessed | tf_op | source)
XLA Modules:
  0.0 242.6 jit_solution(920060485825970964)
XLA Ops:
  8.9 1.6 reshape.157
  11.9 5.2 %reduce-window.6 = s32[8,26,128]{2,1,0:T(8,128)} reduce-window(s32[8,26,128]{2,1,0:T(8,128)} %fusion.17, s32[]{:T(128)} %constant.10.clone.1), window={size=1x1x128 pad=0_0x0_0x127_0}, to_apply=%region_0.0 | reduce-window | flops 3381248 | bytes 212996 | tf_op jit(solution)/shard_map/reduce-window
  17.1 1.8 slice_reduce_fusion
  18.9 1.5 reduce-window.9
  22.2 13.5 %scatter_custom_fusion = s32[4992]{0:T(1024)} fusion(s32[3328]{0:T(1024)S(1)} %fusion.22, s32[3328]{0:T(1024)} %reshape.157, s32[]{:T(128)} %constant.10.clone.1), kind=kCustom, calls=%fused_computation.40 | custom fusion | bytes 20480 | tf_op jit(solution)/shard_map/scatter | solution.py:37
  37.1 9.9 %all_to_all.22 = s32[8,1,624]{2,1,0:T(1,128)S(1)} all-to-all(s32[8,1,624]{2,1,0:T(1,128)} %all_to_all.14), channel_id=1, replica_groups=mesh['grp'=4,'emb'=8] {'emb'}, dimensions={0} | all-to-all | bytes 39936 | tf_op jit(solution)/shard_map/all_to_all | solution.py:39
  51.1 12.3 %gather_fusion = bf16[4992,128]{1,0:T(8,128)(2,1)} fusion(bf16[2496,128]{1,0:T(8,128)(2,1)} %bitcast.32, s32[5120]{0:T(1024)} %pad_clamp_fusion), kind=kCustom, calls=%fused_computation | custom fusion | bytes 2575872 | tf_op jit(solution)/shard_map/gather | solution.py:40
  63.4 4.3 %all-to-all-start.1 = ((bf16[8,624,128]{2,1,0:T(8,128)(2,1)}), bf16[8,624,128]{2,1,0:T(8,128)(2,1)}, u32[]{:S(2)}, u32[]{:S(2)}) async-start(bf16[8,624,128]{2,1,0:T(8,128)(2,1)} %bitcast.34), calls=%async_computation.1 | async-start | bytes 2555904 | tf_op jit(solution)/shard_map/all_to_all | solution.py:41
  72.3 13.2 %all-to-all-done.1 = bf16[8,624,128]{2,1,0:T(8,128)(2,1)} async-done(((bf16[8,624,128]{2,1,0:T(8,128)(2,1)}), bf16[8,624,128]{2,1,0:T(8,128)(2,1)}, u32[]{:S(2)}, u32[]{:S(2)}) %all-to-all-start.1) | async-done | bytes 1277984 | tf_op jit(solution)/shard_map/all_to_all | solution.py:41
  85.5 9.2 %gather_fusion.1 = bf16[3328,128]{1,0:T(8,128)(2,1)} fusion(bf16[4992,128]{1,0:T(8,128)(2,1)} %bitcast.4, s32[4096]{0:T(1024)} %pad_clamp_fusion.1), kind=kCustom, calls=%fused_computation.1 | custom fusion | bytes 1717248 | tf_op jit(solution)/shard_map/gather | solution.py:42
  94.7 2.8 %reshape.131 = bf16[128,3328]{1,0:T(8,128)(2,1)} reshape(bf16[3328,128]{1,0:T(8,128)(2,1)} %gather_fusion.1) | data formatting | bytes 1703936 | tf_op jit(solution)/shard_map/reshape | solution.py:42
  97.5 2.1 constant_dynamic-update-slice_fusion
  99.6 5.6 %fusion.6 = (f32[128]{0:T(128)}, f32[128,3456]{1,0:T(8,128)}) fusion(bf16[128,3456]{1,0:T(8,128)(2,1)} %constant_dynamic-update-slice_fusion, f32[3456]{0:T(1024)S(1)} %convert_element_type.40, f32[3456]{0:T(1024)} %param.19, bf16[512,3456]{1,0:T(8,128)(2,1)} %param.18, bf16[3456,512]{1,0:T(8,128)(2,1)S(1)} %copy-done), kind=kOutput, calls=%fused_computation.16 | convolution fusion | flops 908689280 | bytes 9760256 | tf_op jit(solution)/shard_map/dot_general | solution.py:49
  106.4 6.1 %fusion = bf16[128,3456]{1,0:T(8,128)(2,1)} fusion(bf16[3456,512]{1,0:T(8,128)(2,1)S(1)} %copy-done, f32[128,3456]{1,0:T(8,128)} %get-tuple-element.4, bf16[512,3456]{1,0:T(8,128)(2,1)} %param.18, bf16[128,3456]{1,0:T(8,128)(2,1)} %constant_dynamic-update-slice_fusion, f32[128]{0:T(128)} %divide_subtract_fusion, f32[3456]{0:T(1024)S(1)} %convert_element_type.40), kind=kOutput, calls=%fused_computation.7 | convolution fusion | flops 910016512 | bytes 10631168 | tf_op jit(solution)/shard_map/dot_general | solution.py:66
  112.4 2.1 slice.21
  114.5 2.9 %reshape.165 = bf16[3328,128]{1,0:T(8,128)(2,1)} reshape(bf16[128,3328]{1,0:T(8,128)(2,1)} %slice.21) | data formatting | bytes 1703936 | tf_op jit(solution)/shard_map/reshape | solution.py:71
  117.4 14.9 %scatter_custom_fusion.1 = bf16[4992,128]{1,0:T(8,128)(2,1)} fusion(s32[3328]{0:T(1024)} %copy-done.2, bf16[3328,128]{1,0:T(8,128)(2,1)} %reshape.165, bf16[]{:T(256)} %constant.5.clone.1), kind=kCustom, calls=%fused_computation.21 | custom fusion | bytes 1278464 | tf_op jit(solution)/shard_map/scatter | solution.py:73
  132.3 4.3 %all-to-all-start.2 = ((bf16[8,624,128]{2,1,0:T(8,128)(2,1)}), bf16[8,624,128]{2,1,0:T(8,128)(2,1)}, u32[]{:S(2)}, u32[]{:S(2)}) async-start(bf16[8,624,128]{2,1,0:T(8,128)(2,1)} %bitcast.33), calls=%async_computation.2 | async-start | bytes 2555904 | tf_op jit(solution)/shard_map/all_to_all | solution.py:75
  141.0 13.4 %all-to-all-done.2 = bf16[8,624,128]{2,1,0:T(8,128)(2,1)} async-done(((bf16[8,624,128]{2,1,0:T(8,128)(2,1)}), bf16[8,624,128]{2,1,0:T(8,128)(2,1)}, u32[]{:S(2)}, u32[]{:S(2)}) %all-to-all-start.2) | async-done | bytes 1277984 | tf_op jit(solution)/shard_map/all_to_all | solution.py:75
  154.4 33.9 %scatter_custom_fusion.2 = f32[2496,128]{1,0:T(8,128)} fusion(s32[4992]{0:T(1024)} %fusion.21, bf16[4992,128]{1,0:T(8,128)(2,1)} %bitcast.8, f32[]{:T(128)} %constant.9.clone.1), kind=kCustom, calls=%fused_computation.9 | custom fusion | flops 1277952 | bytes 2556416 | tf_op jit(solution)/shard_map/scatter-add | solution.py:85
  188.4 2.2 convert_element_type.47
  192.0 2.1 fusion.3
  194.1 39.5 %psum.15 = f32[3456]{0:T(1024)} all-reduce(f32[3456]{0:T(1024)} %fusion.3), channel_id=1, replica_groups=mesh['grp'=4,'emb'=8] {'grp','emb'}, use_global_device_ids=true, to_apply=%region_10.11 | all-reduce | flops 3456 | bytes 27648 | tf_op jit(solution)/shard_map/psum | solution.py:90
  233.5 2.3 reshape.135
  (30 shorter events, 22.1 us)
Async XLA Ops:
  7.2 92.5 %copy-start = (bf16[3456,512]{1,0:T(8,128)(2,1)S(1)}, bf16[3456,512]{1,0:T(8,128)(2,1)}, u32[]{:S(2)}) copy-start(bf16[3456,512]{1,0:T(8,128)(2,1)} %param.17) | copy-start | bytes 10616836
  22.2 41.2 %copy-start.2 = (s32[3328]{0:T(1024)}, s32[3328]{0:T(1024)S(1)}, u32[]{:S(2)}) copy-start(s32[3328]{0:T(1024)S(1)} %fusion.22) | copy-start | bytes 39940
  47.1 0.6 copy-start.1
  63.4 22.1 %all-to-all-start.1 = ((bf16[8,624,128]{2,1,0:T(8,128)(2,1)}), bf16[8,624,128]{2,1,0:T(8,128)(2,1)}, u32[]{:S(2)}, u32[]{:S(2)}) async-start(bf16[8,624,128]{2,1,0:T(8,128)(2,1)} %bitcast.34), calls=%async_computation.1 | async-start | bytes 2555904 | tf_op jit(solution)/shard_map/all_to_all | solution.py:41
  132.3 22.1 %all-to-all-start.2 = ((bf16[8,624,128]{2,1,0:T(8,128)(2,1)}), bf16[8,624,128]{2,1,0:T(8,128)(2,1)}, u32[]{:S(2)}, u32[]{:S(2)}) async-start(bf16[8,624,128]{2,1,0:T(8,128)(2,1)} %bitcast.33), calls=%async_computation.2 | async-start | bytes 2555904 | tf_op jit(solution)/shard_map/all_to_all | solution.py:75
  136.5 97.0 %all-reduce.2.cloned.1.call-start = ((), (), s32[]{:S(2)}) async-start(), calls=%async_computation.3 | async-start | bytes 1277952 | tf_op jit(solution)/shard_map/psum | solution.py:87
Sparse Core Ops, SparseCore 0:
  190.7 39.9 all-reduce.1
where the time goes:
time: 245 us; the launch traced here: 243 us
  local copies, waits for them, and re-layouts  71.5 us (29%)
  other arithmetic  60.6 us (25%)
  blocking collectives  49.4 us (20%)
  waiting for transfers between devices  26.7 us (11%)
  between operations  14.1 us (6%)
  matrix products  11.6 us (5%)
  starting transfers between devices  8.73 us (4%)
    psum x1, blocking collectives, local(): bias_grad = lax.psum(bias_local, ('grp', 'emb'))  39.5 us
    scatter-add x1, other arithmetic, local(): local_grad = jnp.zeros((table_count * rows_local, row_width), jnp.float32...  33.9 us
    scatter x1, local copies, waits for them, and re-layouts, local(): jnp.zeros((owner_count * capacity, row_width), jnp.bfloat16)  14.9 us
    scatter x1, local copies, waits for them, and re-layouts, local(): jnp.zeros((owner_count * capacity,), jnp.int32).at[buffer_place]  13.5 us
    all_to_all x1, waiting for transfers between devices, local(): lax.all_to_all(outgoing.reshape(owner_count, capacity, row_width), 'emb',...  13.4 us
    all_to_all x1, waiting for transfers between devices, local(): lax.all_to_all(fetched, 'emb', split_axis=0, concat_axis=0, tiled=True)  13.2 us
    gather x1, local copies, waits for them, and re-layouts, local(): fetched = flat_table[received]  12.3 us
    all_to_all x1, blocking collectives, local(): lax.all_to_all(request, 'emb', split_axis=0, concat_axis=0, tiled=True)  9.94 us
  transfers between devices with their start and end apart: 3, of which 2 were waited for; matrix products, arithmetic and copies ran while one was open for 5% of the time, Pallas kernels for 0%

commit v1 on v0

--- a/solution.py
+++ b/solution.py
@@ -2,6 +2,36 @@
 import jax.numpy as jnp
 from jax import lax
 from jax.sharding import PartitionSpec as P
+
+
+def manage_trees(patch, where_dim, s0):
+    outcome_arr, r_now = (patch.shape[:where_dim], patch.shape[where_dim + 1 :])
+    aux = patch.reshape(*outcome_arr, s0, -1, *r_now)
+    return jnp.moveaxis(aux, where_dim, 0)
+
+
+def _lift_rails(content, out_dim):
+    content = jnp.moveaxis(content, 0, out_dim)
+    clean = content.shape
+    return content.reshape(
+        *clean[:out_dim], clean[out_dim] * clean[out_dim + 1], *clean[out_dim + 2 :]
+    )
+
+
+def clusters_spread(t0, axis_id, xx, frame_in):
+    side_arr, mixed_arr = (lax.axis_size(axis_id), lax.axis_index(axis_id))
+    local_now = manage_trees(t0, xx, side_arr)
+    seen_now = local_now
+    for i in range(1, side_arr):
+        long_array, passed = ((mixed_arr + i) % side_arr, (mixed_arr - i) % side_arr)
+        state_now = lax.dynamic_index_in_dim(local_now, long_array, 0)
+        prior = lax.ppermute(
+            state_now,
+            axis_name=axis_id,
+            perm=tuple(((h, (h + i) % side_arr) for h in range(side_arr))),
+        )
+        seen_now = lax.dynamic_update_slice_in_dim(seen_now, prior, passed, axis=0)
+    return _lift_rails(seen_now, frame_in)
 
 
 def local(
@@ -38,7 +68,7 @@
     request = request.reshape(owner_count, capacity)
     received = lax.all_to_all(request, "emb", split_axis=0, concat_axis=0, tiled=True)
     fetched = flat_table[received]
-    arrived = lax.all_to_all(fetched, "emb", split_axis=0, concat_axis=0, tiled=True)
+    arrived = clusters_spread(fetched, "emb", 0, frame_in=0)
     pooled = arrived.reshape(owner_count * capacity, row_width)[buffer_place].reshape(
         sample_count, table_count * row_width
     )

time: 245 us -> 248 us (1.012)
  blocking collectives: 49.4 us -> 39.5 us
  starting transfers between devices: 8.73 us -> 18.1 us
  local copies, waits for them, and re-layouts: 71.5 us -> 79.7 us
  waiting for transfers between devices: 26.7 us -> 20.7 us
    all_to_all x1 -> x0, blocking collectives: 9.94 us -> none  [local(): lax.all_to_all(request, 'emb', split_axis=0, concat_axis=0, tiled=True)]
    all_to_all x1, waiting for transfers between devices: 13.2 us -> 3.6 us  [local(): lax.all_to_all(request, 'emb', split_axis=0, concat_axis=0, tiled=True)]
    dynamic_update_slice x0 -> x7, local copies, waits for them, and re-layouts: none -> 6.55 us  [clusters_spread(): seen_now = lax.dynamic_update_slice_in_dim(seen_now, prior, passed, axis=0)]
    ppermute x0 -> x7, starting transfers between devices: none -> 6.38 us  [clusters_spread(): lax.ppermute(state_now, axis_name=axis_id, perm=tuple(((h, (h + i) % side...]
    ppermute x0 -> x7, waiting for transfers between devices: none -> 3.12 us  [clusters_spread(): lax.ppermute(state_now, axis_name=axis_id, perm=tuple(((h, (h + i) % side...]
  transfers between devices with their start and end apart: 3 -> 10, of which waited for: 2 -> 5; matrix products, arithmetic and copies ran while one was open for 5% -> 7% of each run, Pallas kernels for 0% -> 0%
where the time goes in v1:
time: 248 us; the launch traced here: 246 us
  local copies, waits for them, and re-layouts  79.7 us (32%)
  other arithmetic  61.9 us (25%)
  blocking collectives  39.5 us (16%)
  waiting for transfers between devices  20.7 us (8%)
  starting transfers between devices  18.1 us (7%)
  between operations  14.1 us (6%)
  matrix products  11.6 us (5%)
    psum x1, blocking collectives, local(): bias_grad = lax.psum(bias_local, ('grp', 'emb'))  39.5 us
    scatter-add x1, other arithmetic, local(): local_grad = jnp.zeros((table_count * rows_local, row_width), jnp.float32...  33.9 us
    scatter x1, local copies, waits for them, and re-layouts, local(): jnp.zeros((owner_count * capacity, row_width), jnp.bfloat16)  14.9 us
    all_to_all x1, waiting for transfers between devices, local(): lax.all_to_all(outgoing.reshape(owner_count, capacity, row_width), 'emb',...  13.9 us
    scatter x1, local copies, waits for them, and re-layouts, local(): jnp.zeros((owner_count * capacity,), jnp.int32).at[buffer_place]  13.5 us
    gather x1, local copies, waits for them, and re-layouts, local(): fetched = flat_table[received]  12.3 us
    gather x1, local copies, waits for them, and re-layouts, local(): arrived.reshape(owner_count * capacity, row_width)[buffer_place]  9.15 us
    another operation x2, other arithmetic  6.68 us
  transfers between devices with their start and end apart: 10, of which 5 were waited for; matrix products, arithmetic and copies ran while one was open for 7% of the time, Pallas kernels for 0%

profile of v1, /device:TPU:0, one launch (start us, length us, event | category | flops | bytes accessed | tf_op | source)
XLA Modules:
  0.0 245.5 jit_solution(3279798971399338717)
XLA Ops:
  9.4 5.2 %reduce-window.6 = s32[8,26,128]{2,1,0:T(8,128)} reduce-window(s32[8,26,128]{2,1,0:T(8,128)} %fusion.17, s32[]{:T(128)} %constant.117.clone.1), window={size=1x1x128 pad=0_0x0_0x127_0}, to_apply=%region_0.0 | reduce-window | flops 3381248 | bytes 212996 | tf_op jit(solution)/shard_map/reduce-window
  14.6 1.8 slice_reduce_fusion
  24.1 13.5 %scatter_custom_fusion = s32[4992]{0:T(1024)} fusion(s32[3328]{0:T(1024)S(1)} %fusion.22, s32[3328]{0:T(1024)} %reshape.164, s32[]{:T(128)} %constant.117.clone.1), kind=kCustom, calls=%fused_computation.47 | custom fusion | bytes 20480 | tf_op jit(solution)/shard_map/scatter | solution.py:67
  39.0 5.2 %all-to-all-start = ((s32[8,1,624]{2,1,0:T(1,128)}), s32[8,1,624]{2,1,0:T(1,128)}, u32[]{:S(2)}, u32[]{:S(2)}) async-start(s32[8,1,624]{2,1,0:T(1,128)} %all_to_all.11), calls=%async_computation | async-start | bytes 40960 | tf_op jit(solution)/shard_map/all_to_all | solution.py:69
  45.5 3.6 %all-to-all-done = s32[8,1,624]{2,1,0:T(1,128)} async-done(((s32[8,1,624]{2,1,0:T(1,128)}), s32[8,1,624]{2,1,0:T(1,128)}, u32[]{:S(2)}, u32[]{:S(2)}) %all-to-all-start) | async-done | bytes 20000 | tf_op jit(solution)/shard_map/all_to_all | solution.py:69
  53.2 12.3 %gather_fusion = bf16[4992,128]{1,0:T(8,128)(2,1)} fusion(bf16[2496,128]{1,0:T(8,128)(2,1)} %bitcast.45, s32[5120]{0:T(1024)} %pad_clamp_fusion), kind=kCustom, calls=%fused_computation | custom fusion | bytes 2575872 | tf_op jit(solution)/shard_map/gather | solution.py:70
  65.5 2.3 dynamic-slice_bitcast_fusion
  75.7 1.6 constant_dynamic-update-slice_fusion.8
  80.3 1.8 collective-permute-done.2
  85.9 9.2 %gather_fusion.1 = bf16[3328,128]{1,0:T(8,128)(2,1)} fusion(bf16[4992,128]{1,0:T(8,128)(2,1)} %bitcast.48, s32[4096]{0:T(1024)} %pad_clamp_fusion.1), kind=kCustom, calls=%fused_computation.1 | custom fusion | bytes 1717248 | tf_op jit(solution)/shard_map/gather | solution.py:72
  95.0 2.8 %reshape.138 = bf16[128,3328]{1,0:T(8,128)(2,1)} reshape(bf16[3328,128]{1,0:T(8,128)(2,1)} %gather_fusion.1) | data formatting | bytes 1703936 | tf_op jit(solution)/shard_map/reshape | solution.py:72
  97.8 2.1 constant_dynamic-update-slice_fusion
  99.9 5.6 %fusion.6 = (f32[128]{0:T(128)}, f32[128,3456]{1,0:T(8,128)}) fusion(bf16[128,3456]{1,0:T(8,128)(2,1)} %constant_dynamic-update-slice_fusion, f32[3456]{0:T(1024)S(1)} %convert_element_type.40, f32[3456]{0:T(1024)} %param.19, bf16[512,3456]{1,0:T(8,128)(2,1)} %param.18, bf16[3456,512]{1,0:T(8,128)(2,1)S(1)} %copy-done), kind=kOutput, calls=%fused_computation.16 | convolution fusion | flops 908689280 | bytes 9760256 | tf_op jit(solution)/shard_map/dot_general | solution.py:79
  106.7 6.1 %fusion = bf16[128,3456]{1,0:T(8,128)(2,1)} fusion(bf16[3456,512]{1,0:T(8,128)(2,1)S(1)} %copy-done, f32[128,3456]{1,0:T(8,128)} %get-tuple-element.11, bf16[512,3456]{1,0:T(8,128)(2,1)} %param.18, bf16[128,3456]{1,0:T(8,128)(2,1)} %constant_dynamic-update-slice_fusion, f32[128]{0:T(128)} %divide_subtract_fusion, f32[3456]{0:T(1024)S(1)} %convert_element_type.40), kind=kOutput, calls=%fused_computation.7 | convolution fusion | flops 910016512 | bytes 10631168 | tf_op jit(solution)/shard_map/dot_general | solution.py:96
  112.8 2.1 slice.21
  114.9 2.9 %reshape.172 = bf16[3328,128]{1,0:T(8,128)(2,1)} reshape(bf16[128,3328]{1,0:T(8,128)(2,1)} %slice.21) | data formatting | bytes 1703936 | tf_op jit(solution)/shard_map/reshape | solution.py:101
  117.8 14.9 %scatter_custom_fusion.1 = bf16[4992,128]{1,0:T(8,128)(2,1)} fusion(s32[3328]{0:T(1024)} %copy-done.1, bf16[3328,128]{1,0:T(8,128)(2,1)} %reshape.172, bf16[]{:T(256)} %constant.123.clone.1), kind=kCustom, calls=%fused_computation.21 | custom fusion | bytes 1278464 | tf_op jit(solution)/shard_map/scatter | solution.py:103
  132.6 6.5 %all-to-all-start.1 = ((bf16[8,624,128]{2,1,0:T(8,128)(2,1)}), bf16[8,624,128]{2,1,0:T(8,128)(2,1)}, u32[]{:S(2)}, u32[]{:S(2)}) async-start(bf16[8,624,128]{2,1,0:T(8,128)(2,1)} %bitcast.49), calls=%async_computation.1 | async-start | bytes 2555904 | tf_op jit(solution)/shard_map/all_to_all | solution.py:105
  143.4 13.9 %all-to-all-done.1 = bf16[8,624,128]{2,1,0:T(8,128)(2,1)} async-done(((bf16[8,624,128]{2,1,0:T(8,128)(2,1)}), bf16[8,624,128]{2,1,0:T(8,128)(2,1)}, u32[]{:S(2)}, u32[]{:S(2)}) %all-to-all-start.1) | async-done | bytes 1277984 | tf_op jit(solution)/shard_map/all_to_all | solution.py:105
  157.3 33.9 %scatter_custom_fusion.2 = f32[2496,128]{1,0:T(8,128)} fusion(s32[4992]{0:T(1024)} %fusion.21, bf16[4992,128]{1,0:T(8,128)(2,1)} %bitcast.16, f32[]{:T(128)} %constant.116.clone.1), kind=kCustom, calls=%fused_computation.9 | custom fusion | flops 1277952 | bytes 2556416 | tf_op jit(solution)/shard_map/scatter-add | solution.py:115
  191.2 2.2 convert_element_type.47
  194.8 2.1 fusion.3
  196.9 39.5 %psum.15 = f32[3456]{0:T(1024)} all-reduce(f32[3456]{0:T(1024)} %fusion.3), channel_id=1, replica_groups=mesh['grp'=4,'emb'=8] {'grp','emb'}, use_global_device_ids=true, to_apply=%region_10.11 | all-reduce | flops 3456 | bytes 27648 | tf_op jit(solution)/shard_map/psum | solution.py:120
  236.4 2.3 reshape.142
  (51 shorter events, 38.2 us)
Async XLA Ops:
  7.2 92.8 %copy-start = (bf16[3456,512]{1,0:T(8,128)(2,1)S(1)}, bf16[3456,512]{1,0:T(8,128)(2,1)}, u32[]{:S(2)}) copy-start(bf16[3456,512]{1,0:T(8,128)(2,1)} %param.17) | copy-start | bytes 10616836
  19.7 49.4 %copy-start.1 = (s32[3328]{0:T(1024)}, s32[3328]{0:T(1024)S(1)}, u32[]{:S(2)}) copy-start(s32[3328]{0:T(1024)S(1)} %fusion.22) | copy-start | bytes 39940
  39.0 10.1 %all-to-all-start = ((s32[8,1,624]{2,1,0:T(1,128)}), s32[8,1,624]{2,1,0:T(1,128)}, u32[]{:S(2)}, u32[]{:S(2)}) async-start(s32[8,1,624]{2,1,0:T(1,128)} %all_to_all.11), calls=%async_computation | async-start | bytes 40960 | tf_op jit(solution)/shard_map/all_to_all | solution.py:69
  65.5 2.3 copy-start.2
  67.9 6.4 %collective-permute-start = (bf16[1,1,624,128]{3,2,0,1:T(8,128)(2,1)}, bf16[1,1,624,128]{3,2,0,1:T(8,128)(2,1)}, u32[]{:S(2)}, u32[]{:S(2)}) collective-permute-start(bf16[1,1,624,128]{3,2,0,1:T(8,128)(2,1)} %get-tuple-element.8), channel_id=1, source_target_pairs={{0,1},{1,2},{2,3},{3,4},{4,5},{5,6},{6,7},{7,0},{8,9},{9,10},{10,1... | collective-permute-start | bytes 479240 | tf_op jit(solution)/shard_map/ppermute | solution.py:28
  68.5 8.8 %collective-permute-start.1 = (bf16[1,1,624,128]{3,2,0,1:T(8,128)(2,1)}, bf16[1,1,624,128]{3,2,0,1:T(8,128)(2,1)}, u32[]{:S(2)}, u32[]{:S(2)}) collective-permute-start(bf16[1,1,624,128]{3,2,0,1:T(8,128)(2,1)} %get-tuple-element.7), channel_id=1, source_target_pairs={{0,2},{1,3},{2,4},{3,5},{4,6},{5,7},{6,0},{7,1},{8,10},{9,11},{10,... | collective-permute-start | bytes 479240 | tf_op jit(solution)/shard_map/ppermute | solution.py:28
  70.4 11.7 %collective-permute-start.2 = (bf16[1,1,624,128]{3,2,0,1:T(8,128)(2,1)}, bf16[1,1,624,128]{3,2,0,1:T(8,128)(2,1)S(1)}, u32[]{:S(2)}, u32[]{:S(2)}) collective-permute-start(bf16[1,1,624,128]{3,2,0,1:T(8,128)(2,1)} %get-tuple-element.6), channel_id=1, source_target_pairs={{0,3},{1,4},{2,5},{3,6},{4,7},{5,0},{6,1},{7,2},{8,11},{9,12},{10,... | collective-permute-start | bytes 479240 | tf_op jit(solution)/shard_map/ppermute | solution.py:28
  71.8 11.0 %collective-permute-start.3 = (bf16[1,1,624,128]{3,2,0,1:T(8,128)(2,1)}, bf16[1,1,624,128]{3,2,0,1:T(8,128)(2,1)S(1)}, u32[]{:S(2)}, u32[]{:S(2)}) collective-permute-start(bf16[1,1,624,128]{3,2,0,1:T(8,128)(2,1)} %get-tuple-element.5), channel_id=1, source_target_pairs={{0,4},{1,5},{2,6},{3,7},{4,0},{5,1},{6,2},{7,3},{8,12},{9,13},{10,... | collective-permute-start | bytes 479240 | tf_op jit(solution)/shard_map/ppermute | solution.py:28
  73.3 10.5 %collective-permute-start.4 = (bf16[1,1,624,128]{3,2,0,1:T(8,128)(2,1)}, bf16[1,1,624,128]{3,2,0,1:T(8,128)(2,1)S(1)}, u32[]{:S(2)}, u32[]{:S(2)}) collective-permute-start(bf16[1,1,624,128]{3,2,0,1:T(8,128)(2,1)} %get-tuple-element.4), channel_id=1, source_target_pairs={{0,5},{1,6},{2,7},{3,0},{4,1},{5,2},{6,3},{7,4},{8,13},{9,14},{10,... | collective-permute-start | bytes 479240 | tf_op jit(solution)/shard_map/ppermute | solution.py:28
  74.2 10.3 %collective-permute-start.5 = (bf16[1,1,624,128]{3,2,0,1:T(8,128)(2,1)}, bf16[1,1,624,128]{3,2,0,1:T(8,128)(2,1)S(1)}, u32[]{:S(2)}, u32[]{:S(2)}) collective-permute-start(bf16[1,1,624,128]{3,2,0,1:T(8,128)(2,1)} %get-tuple-element.9), channel_id=1, source_target_pairs={{0,6},{1,7},{2,0},{3,1},{4,2},{5,3},{6,4},{7,5},{8,14},{9,15},{10,... | collective-permute-start | bytes 479240 | tf_op jit(solution)/shard_map/ppermute | solution.py:28
  77.3 7.9 %collective-permute-start.6 = (bf16[1,1,624,128]{3,2,0,1:T(8,128)(2,1)}, bf16[1,1,624,128]{3,2,0,1:T(8,128)(2,1)S(1)}, u32[]{:S(2)}, u32[]{:S(2)}) collective-permute-start(bf16[1,1,624,128]{3,2,0,1:T(8,128)(2,1)} %get-tuple-element.3), channel_id=1, source_target_pairs={{0,7},{1,0},{2,1},{3,2},{4,3},{5,4},{6,5},{7,6},{8,15},{9,8},{10,9... | collective-permute-start | bytes 479240 | tf_op jit(solution)/shard_map/ppermute | solution.py:28
  132.6 24.7 %all-to-all-start.1 = ((bf16[8,624,128]{2,1,0:T(8,128)(2,1)}), bf16[8,624,128]{2,1,0:T(8,128)(2,1)}, u32[]{:S(2)}, u32[]{:S(2)}) async-start(bf16[8,624,128]{2,1,0:T(8,128)(2,1)} %bitcast.49), calls=%async_computation.1 | async-start | bytes 2555904 | tf_op jit(solution)/shard_map/all_to_all | solution.py:105
  139.1 97.3 %all-reduce.2.cloned.1.call-start = ((), (), s32[]{:S(2)}) async-start(), calls=%async_computation.2 | async-start | bytes 1277952 | tf_op jit(solution)/shard_map/psum | solution.py:117
Sparse Core Ops, SparseCore 0:
  193.6 39.9 all-reduce.1
